TPU v7x, 32 devices: a whole 2x2x4 slice. The times are simulated.
32 devices in a mesh: seq: 8 (over y, x, core), fsdp: 4 (over z).
Axes of the slice: x: 2, y: 2, z: 4, core: 2. Of those that a mesh axis runs over, the one named last changes fastest.
Arguments:
- query_states: bfloat16 [2048, 4096], P('seq', 'fsdp'), may hold values from -24 to 24
- key_states: bfloat16 [2048, 4096], P('seq', 'fsdp'), may hold values from -6 to 6
- value_states: bfloat16 [2048, 4096], P('seq', 'fsdp'), may hold values from -6 to 6
- positions: int32 [2048], P('seq'), may hold values from 0 to 2047, as said below
- out_weight: bfloat16 [4096, 5120], P('fsdp', 'seq'), may hold values from -1 to 1
- cotangent: bfloat16 [2048, 5120], P('seq', 'fsdp'), may hold values from -0.59765625 to 0.59765625
Outputs:
- attn_output: float32 [2048, 5120], P('seq', 'fsdp')
- grad_queries: float32 [2048, 4096], P('seq', 'fsdp')
- grad_keys: float32 [2048, 4096], P('seq', 'fsdp')
- grad_values: float32 [2048, 4096], P('seq', 'fsdp')
- grad_weight: float32 [4096, 5120], P('fsdp', 'seq')
Inputs may be any that keep to these rules, and one draw needn't show every extreme that they name: A permutation of 0 to 2047; each aligned block of 256 rows holds, in increasing order, the positions of one residue class modulo 2048 // 256.
All inputs are finite; a program needn't handle non-finite values.
Results may differ from a plain program's by a relative error of at most 0.02.
Values may be sent and summed in bfloat16 or wider, within the bound.
No kernel may reach another device: no remote copies, remote signals or barrier semaphores. Data moves between devices by JAX's collectives and lax.ppermute only.
A program may use at most 128 MiB of HBM per device.

v0:
```python
import jax
import jax.numpy as jnp
from jax import lax
from jax.sharding import PartitionSpec as P

HEAD_DIM = 128
blocked = -1e30


def split_heads(matrix):
    return matrix.reshape(matrix.shape[0], -1, HEAD_DIM)


def masked_scores(query_rows, key_rows, query_pos, key_pos):
    raw = jnp.einsum(
        "qhd,khd->hqk", query_rows, key_rows, preferred_element_type=jnp.float32
    ) * HEAD_DIM ** (-0.5)
    visible = key_pos[None, None, :] <= query_pos[None, :, None]
    return jnp.where(visible, raw, blocked)


def shards(query_states, key_states, value_states, positions, out_weight, cotangent):
    local_tokens = query_states.shape[0]
    query_heads = split_heads(query_states)
    local_heads = query_heads.shape[1]
    all_keys = lax.all_gather(key_states, "seq", axis=0, tiled=True)
    all_values = lax.all_gather(value_states, "seq", axis=0, tiled=True)
    all_pos = lax.all_gather(positions, "seq", axis=0, tiled=True)
    key_heads = split_heads(all_keys)
    value_heads = split_heads(all_values)
    scores = masked_scores(query_heads, key_heads, positions, all_pos)
    row_max = jnp.max(scores, axis=2)
    log_total = row_max + jnp.log(jnp.sum(jnp.exp(scores - row_max[:, :, None]), axis=2))
    probs = jnp.exp(scores - log_total[:, :, None])
    weights = probs.astype(jnp.bfloat16)
    attended = jnp.einsum("hqk,khd->qhd", weights, value_heads, preferred_element_type=jnp.float32)
    attended_heads = attended.astype(jnp.bfloat16)
    attended_flat = attended_heads.reshape(local_tokens, local_heads * HEAD_DIM)
    weight_full = lax.all_gather(out_weight, "seq", axis=1, tiled=True)
    partial_sum = jnp.dot(attended_flat, weight_full, preferred_element_type=jnp.float32).astype(
        jnp.bfloat16
    )
    attn_output = lax.psum_scatter(partial_sum, "fsdp", scatter_dimension=1, tiled=True).astype(
        jnp.float32
    )
    cotangent_full = lax.all_gather(cotangent, "fsdp", axis=1, tiled=True)
    grad_attended = jnp.einsum(
        "td,hd->th", cotangent_full, weight_full, preferred_element_type=jnp.float32
    ).astype(jnp.bfloat16)
    all_attended = lax.all_gather(attended_flat, "seq", axis=0, tiled=True)
    cotangent_cols = lax.all_to_all(cotangent_full, "seq", 1, 0, tiled=True)
    grad_weight = jnp.einsum(
        "th,td->hd", all_attended, cotangent_cols, preferred_element_type=jnp.float32
    )
    grad_heads = split_heads(grad_attended)
    row_delta = jnp.sum(
        grad_heads.astype(jnp.float32) * attended_heads.astype(jnp.float32), axis=2
    ).T
    grad_probs = jnp.einsum(
        "qhd,khd->hqk", grad_heads, value_heads, preferred_element_type=jnp.float32
    )
    grad_scores = (probs * (grad_probs - row_delta[:, :, None])).astype(jnp.bfloat16)
    query_sum = jnp.einsum(
        "hqk,khd->qhd", grad_scores, key_heads, preferred_element_type=jnp.float32
    )
    key_part = jnp.einsum(
        "hqk,qhd->khd", grad_scores, query_heads, preferred_element_type=jnp.float32
    )
    value_part = jnp.einsum("hqk,qhd->khd", weights, grad_heads, preferred_element_type=jnp.float32)
    key_sum = lax.psum_scatter(key_part, "seq", scatter_dimension=0, tiled=True)
    value_sum = lax.psum_scatter(value_part, "seq", scatter_dimension=0, tiled=True)
    score_scale = HEAD_DIM ** (-0.5)
    grad_queries = (query_sum * score_scale).reshape(local_tokens, local_heads * HEAD_DIM)
    grad_keys = (key_sum * score_scale).reshape(local_tokens, local_heads * HEAD_DIM)
    grad_values = value_sum.reshape(local_tokens, local_heads * HEAD_DIM)
    return (attn_output, grad_queries, grad_keys, grad_values, grad_weight)


def solution(mesh):
    in_specs = (
        P("seq", "fsdp"),
        P("seq", "fsdp"),
        P("seq", "fsdp"),
        P("seq"),
        P("fsdp", "seq"),
        P("seq", "fsdp"),
    )
    out_specs = (
        P("seq", "fsdp"),
        P("seq", "fsdp"),
        P("seq", "fsdp"),
        P("seq", "fsdp"),
        P("fsdp", "seq"),
    )
    return jax.shard_map(shards, mesh=mesh, in_specs=in_specs, out_specs=out_specs, check_vma=False)
```

profile of v0, /device:TPU:0, one launch (start us, length us, event | category | flops | bytes accessed | tf_op | source)
XLA Modules:
  0.0 487.9 jit_solution(822385104639132643)
XLA Ops:
  7.2 0.7 all-gather.9.cloned.1.call-update
  8.0 2.0 copy.49
  10.1 2.2 copy.53
  12.9 10.6 %all-gather = s32[8,1,256]{2,1,0:T(1,128)S(1)} all-gather(s32[1,1,256]{2,1,0:T(1,128)} %bitcast.66), channel_id=1, replica_groups=mesh['seq'=8,'fsdp'=4] {'seq'}, dimensions={0}, use_global_device_ids=true | all-gather | bytes 9216 | tf_op jit(solution)/shard_map/all_gather | solution.py:28
  23.5 1.0 broadcast_compare_fusion
  24.5 24.7 %all-gather.9.cloned.1.call-done = bf16[2048,1024]{1,0:T(8,128)(2,1)} async-done(((bf16[256,1024]{1,0:T(8,128)(2,1)}), bf16[2048,1024]{1,0:T(8,128)(2,1)}) %all-gather.9.cloned.1.call-update) | async-done | bytes 4194320 | tf_op jit(solution)/shard_map/all_gather | solution.py:27
  49.2 6.5 %copy.52 = bf16[2048,1024]{0,1:T(8,128)(2,1)} copy(bf16[2048,1024]{1,0:T(8,128)(2,1)} %all-gather.9.cloned.1.call-done) | data formatting | bytes 8388608 | tf_op jit(solution)/shard_map/all_gather | solution.py:27
  55.8 33.3 %all-gather.7.cloned.1.call-done = bf16[2048,1024]{0,1:T(8,128)(2,1)} async-done(((bf16[256,1024]{0,1:T(8,128)(2,1)}), bf16[2048,1024]{0,1:T(8,128)(2,1)}) %all-gather.7.cloned.1.call-update) | async-done | bytes 4194320 | tf_op jit(solution)/shard_map/all_gather | solution.py:26
  89.0 5.3 %fusion.1 = (f32[8,256]{1,0:T(8,128)S(1)}, f32[8,256,2048]{2,1,0:T(8,128)S(1)}) fusion(pred[256,2048]{1,0:T(8,128)(4,1)S(1)} %broadcast_compare_fusion, bf16[2048,8,128]{0,2,1:T(8,128)(2,1)} %bitcast.51, bf16[256,1024]{1,0:T(8,128)(2,1)S(1)} %copy-done), kind=kOutput, calls=%fused_computation.5 | convolution fusion | flops 1086322688 | bytes 22028288 | tf_op jit(solution)/shard_map/qhd,khd->hqk/dot_general | solution.py:15
  94.3 4.5 exponential_reduce_fusion
  98.8 1.7 copy-done.1
  100.5 45.4 %all-gather.13.cloned.1.call-done = bf16[256,5120]{0,1:T(8,128)(2,1)} async-done(((bf16[256,1280]{0,1:T(8,128)(2,1)}), bf16[256,5120]{0,1:T(8,128)(2,1)}) %all-gather.13.cloned.1.call-update) | async-done | bytes 2621456 | tf_op jit(solution)/shard_map/all_gather | solution.py:46
  146.0 63.5 %all-gather.11.cloned.1.call-done = bf16[1024,5120]{1,0:T(8,128)(2,1)} async-done(((bf16[1024,640]{1,0:T(8,128)(2,1)}), bf16[1024,5120]{1,0:T(8,128)(2,1)}) %all-gather.11.cloned.1.call-update) | async-done | bytes 10485776 | tf_op jit(solution)/shard_map/all_gather | solution.py:39
  209.5 7.7 %convolution_convert_fusion.1 = bf16[256,1024]{1,0:T(8,128)(2,1)S(1)} fusion(bf16[256,5120]{0,1:T(8,128)(2,1)} %all-gather.13.cloned.1.call-done, bf16[1024,5120]{1,0:T(8,128)(2,1)} %all-gather.11.cloned.1.call-done), kind=kOutput, calls=%fused_computation.10 | convolution fusion | flops 2684616704 | bytes 13631488 | tf_op jit(solution)/shard_map/td,hd->th/dot_general | solution.py:47
  217.4 9.7 %multiply_reduce_fusion = (f32[256,8]{0,1:T(8,128)S(1)}, bf16[8,256,128]{1,2,0:T(8,128)(2,1)S(1)}) fusion(bf16[256,1024]{0,1:T(8,128)(2,1)S(1)} %copy.54, bf16[2048,8,128]{0,2,1:T(8,128)(2,1)} %bitcast.54, f32[8,256,2048]{2,1,0:T(8,128)} %copy-done.1, f32[8,256]{1,0:T(8,128)S(1)} %log_add_fusion, pred[256,2048]{1,0:T(8,128)(4,1)S(1)} %broadcast_compare_fusion), kind=kOutput, calls=%fused_computation.12 | convolution fusion | flops 1091827712 | bytes 22560768 | tf_op jit(solution)/shard_map/hqk,khd->qhd/dot_general | solution.py:36
  227.1 8.4 %convolution_convert_fusion = bf16[256,5120]{1,0:T(8,128)(2,1)} fusion(bf16[256,1024]{0,1:T(8,128)(2,1)S(1)} %bitcast.57, bf16[1024,5120]{1,0:T(8,128)(2,1)} %all-gather.11.cloned.1.call-done), kind=kOutput, calls=%fused_computation.6 | convolution fusion | flops 2685665280 | bytes 13631488 | tf_op jit(solution)/shard_map/dot_general | solution.py:40
  236.4 11.1 %multiply_convert_fusion = bf16[8,256,2048]{2,1,0:T(8,128)(2,1)S(1)} fusion(f32[8,256,2048]{2,1,0:T(8,128)} %copy-done.1, f32[8,256]{1,0:T(8,128)S(1)} %bitcast.67, f32[8,256]{1,0:T(8,128)S(1)} %log_add_fusion, pred[256,2048]{1,0:T(8,128)(4,1)S(1)} %broadcast_compare_fusion, bf16[256,8,128]{0,2,1:T(8,128)(2,1)S(1)} %bitcast.61, bf16[2048,8,128]{0,2,1:T(8,128)(2,1)} %bitcast.55), kind=kOutput, calls=%fused_computation | convolution fusion | flops 1098907648 | bytes 30425088 | tf_op jit(solution)/shard_map/qhd,khd->hqk/dot_general | solution.py:59
  247.5 3.2 copy-done.2
  250.7 6.0 %convolution_bitcast_fusion.1 = f32[2048,8,128]{2,0,1:T(8,128)} fusion(bf16[8,256,2048]{2,1,0:T(8,128)(2,1)S(1)} %multiply_convert_fusion, bf16[256,1024]{1,0:T(8,128)(2,1)S(1)} %copy-done), kind=kOutput, calls=%fused_computation.8 | convolution fusion | flops 1073741824 | bytes 17301504 | tf_op jit(solution)/shard_map/hqk,qhd->khd/dot_general | solution.py:66
  256.8 10.3 %convolution_bitcast_fusion = f32[2048,8,128]{0,2,1:T(8,128)} fusion(bf16[256,8,128]{0,2,1:T(8,128)(2,1)S(1)} %bitcast.62, f32[8,256,2048]{2,1,0:T(8,128)} %copy-done.1, f32[8,256]{1,0:T(8,128)S(1)} %log_add_fusion, pred[256,2048]{1,0:T(8,128)(4,1)S(1)} %broadcast_compare_fusion), kind=kOutput, calls=%fused_computation.7 | convolution fusion | flops 1090519040 | bytes 26222592 | tf_op jit(solution)/shard_map/hqk,qhd->khd/dot_general | solution.py:69
  267.0 38.1 %all_to_all.19 = bf16[256,8,640]{0,2,1:T(8,128)(2,1)S(1)} all-to-all(bf16[256,8,640]{0,2,1:T(8,128)(2,1)} %bitcast.59), channel_id=1, replica_groups=mesh['seq'=8,'fsdp'=4] {'seq'}, dimensions={1} | all-to-all | bytes 5242880 | tf_op jit(solution)/shard_map/all_to_all | solution.py:51
  305.1 2.6 copy.60
  307.7 8.6 %convolution_multiply_fusion = f32[8,256,128]{1,2,0:T(8,128)} fusion(bf16[8,256,2048]{2,1,0:T(8,128)(2,1)} %copy-done.2, bf16[2048,8,128]{0,2,1:T(8,128)(2,1)} %bitcast.52), kind=kOutput, calls=%fused_computation.9 | convolution fusion | flops 1074003968 | bytes 13631488 | tf_op jit(solution)/shard_map/hqk,khd->qhd/dot_general | solution.py:63
  316.3 2.5 copy.61
  318.9 2.2 convert_element_type.31
  321.1 7.7 %all-gather.15.cloned.1.call-done = bf16[2048,1024]{0,1:T(8,128)(2,1)} async-done(((bf16[256,1024]{0,1:T(8,128)(2,1)}), bf16[2048,1024]{0,1:T(8,128)(2,1)}) %all-gather.15.cloned.1.call-update) | async-done | bytes 4194320 | tf_op jit(solution)/shard_map/all_gather | solution.py:50
  328.8 7.1 %fusion.9 = f32[1024,640]{1,0:T(8,128)} fusion(bf16[2048,1024]{0,1:T(8,128)(2,1)} %all-gather.15.cloned.1.call-done, bf16[2048,640]{1,0:T(8,128)(2,1)S(1)} %bitcast.60), kind=kOutput, calls=%fused_computation.21 | convolution fusion | flops 2684354560 | bytes 9437184 | tf_op jit(solution)/shard_map/th,td->hd/dot_general | solution.py:52
  335.9 67.8 %reduce-scatter.6.cloned.1.call-done = f32[256,8,128]{2,0,1:T(8,128)} async-done(((f32[2048,8,128]{2,0,1:T(8,128)}), f32[256,8,128]{2,0,1:T(8,128)}) %reduce-scatter.6.cloned.1.call-update) | async-done | bytes 1048592 | tf_op jit(solution)/shard_map/reduce_scatter | solution.py:70
  403.7 1.3 broadcast_multiply_fusion
  405.4 1.3 copy.62
  406.7 71.8 %reduce-scatter.8.cloned.1.call-done = f32[256,8,128]{0,2,1:T(8,128)} async-done(((f32[2048,8,128]{0,2,1:T(8,128)}), f32[256,8,128]{0,2,1:T(8,128)}) %reduce-scatter.8.cloned.1.call-update) | async-done | bytes 1048592 | tf_op jit(solution)/shard_map/reduce_scatter | solution.py:71
  478.5 2.5 copy.63
  (27 shorter events, 2.2 us)
Async XLA Ops:
  7.2 81.9 %copy-start = (bf16[256,1024]{1,0:T(8,128)(2,1)S(1)}, bf16[256,1024]{1,0:T(8,128)(2,1)}, u32[]{:S(2)}) copy-start(bf16[256,1024]{1,0:T(8,128)(2,1)} %param.6) | copy-start | bytes 1572868
  7.2 42.0 %all-gather.9.cloned.1.call-start = ((), (), s32[]{:S(2)}) async-start(), calls=%async_computation.5 | async-start | bytes 4718592 | tf_op jit(solution)/shard_map/all_gather | solution.py:27
  7.9 81.1 %all-gather.7.cloned.1.call-start = ((), (), s32[]{:S(2)}) async-start(), calls=%async_computation.4 | async-start | bytes 4718592 | tf_op jit(solution)/shard_map/all_gather | solution.py:26
  10.0 135.9 %all-gather.13.cloned.1.call-start = ((), (), s32[]{:S(2)}) async-start(), calls=%async_computation.8 | async-start | bytes 3276800 | tf_op jit(solution)/shard_map/all_gather | solution.py:46
  12.3 197.2 %all-gather.11.cloned.1.call-start = ((), (), s32[]{:S(2)}) async-start(), calls=%async_computation.6 | async-start | bytes 11796480 | tf_op jit(solution)/shard_map/all_gather | solution.py:39
  12.8 306.0 %reduce-scatter.4.cloned.1.call-start = ((), (), s32[]{:S(2)}) async-start(), calls=%async_computation.7 | async-start | bytes 3276800 | tf_op jit(solution)/shard_map/reduce_scatter | solution.py:43
  94.3 6.2 %copy-start.1 = (f32[8,256,2048]{2,1,0:T(8,128)}, f32[8,256,2048]{2,1,0:T(8,128)S(1)}, u32[]{:S(2)}) copy-start(f32[8,256,2048]{2,1,0:T(8,128)S(1)} %get-tuple-element.26) | copy-start | bytes 50331652
  227.1 8.4 %copy-start.3 = (bf16[8,256,128]{1,2,0:T(8,128)(2,1)}, bf16[8,256,128]{1,2,0:T(8,128)(2,1)S(1)}, u32[]{:S(2)}) copy-start(bf16[8,256,128]{1,2,0:T(8,128)(2,1)S(1)} %get-tuple-element.28) | copy-start | bytes 1572868
  235.6 93.2 %all-gather.15.cloned.1.call-start = ((), (), s32[]{:S(2)}) async-start(), calls=%async_computation.11 | async-start | bytes 4718592 | tf_op jit(solution)/shard_map/all_gather | solution.py:50
  236.1 167.6 %reduce-scatter.6.cloned.1.call-start = ((), (), s32[]{:S(2)}) async-start(), calls=%async_computation.9 | async-start | bytes 9437184 | tf_op jit(solution)/shard_map/reduce_scatter | solution.py:70
  247.5 3.2 copy-start.2
  256.7 221.8 %reduce-scatter.8.cloned.1.call-start = ((), (), s32[]{:S(2)}) async-start(), calls=%async_computation.10 | async-start | bytes 9437184 | tf_op jit(solution)/shard_map/reduce_scatter | solution.py:71
  307.7 21.1 %copy-start.4 = (bf16[8,256,640]{2,1,0:T(8,128)(2,1)S(1)}, bf16[8,256,640]{2,1,0:T(8,128)(2,1)}, u32[]{:S(2)}) copy-start(bf16[8,256,640]{2,1,0:T(8,128)(2,1)} %copy.60) | copy-start | bytes 7864324
Sparse Core Ops, SparseCore 0:
  9.9 39.2 all-gather.8
  51.7 37.3 all-gather.6
  91.2 54.7 all-gather.12
  147.7 61.7 all-gather.10
  235.7 52.2 reduce-scatter.3
  290.3 38.4 all-gather.14
  332.3 71.3 reduce-scatter.5
  407.2 71.2 reduce-scatter.7
where the time goes:
time: 489 us; the launch traced here: 488 us
  waiting for transfers between devices  316 us (65%)
  matrix products  74.1 us (15%)
  blocking collectives  48.6 us (10%)
  local copies, waits for them, and re-layouts  25.2 us (5%)
  between operations  14.3 us (3%)
  other arithmetic  9.09 us (2%)
    reduce_scatter x1, waiting for transfers between devices, shards(): lax.psum_scatter(value_part, 'seq', scatter_dimension=0, tiled=True)  71.8 us
    reduce_scatter x1, waiting for transfers between devices, shards(): key_sum = lax.psum_scatter(key_part, 'seq', scatter_dimension=0, tiled=True)  67.8 us
    all_gather x1, waiting for transfers between devices, shards(): weight_full = lax.all_gather(out_weight, 'seq', axis=1, tiled=True)  63.5 us
    all_gather x1, waiting for transfers between devices, shards(): cotangent_full = lax.all_gather(cotangent, 'fsdp', axis=1, tiled=True)  45.4 us
    all_to_all x1, blocking collectives, shards(): cotangent_cols = lax.all_to_all(cotangent_full, 'seq', 1, 0, tiled=True)  38.1 us
    all_gather x1, waiting for transfers between devices, shards(): all_keys = lax.all_gather(key_states, 'seq', axis=0, tiled=True)  33.3 us
    all_gather x1, waiting for transfers between devices, shards(): all_values = lax.all_gather(value_states, 'seq', axis=0, tiled=True)  24.7 us
    unnamed x15, local copies, waits for them, and re-layouts  15.5 us
  transfers between devices with their start and end apart: 8, of which 7 were waited for; matrix products, arithmetic and copies ran while one was open for 15% of the time, Pallas kernels for 0%

commit v1 on v0

--- a/solution.py
+++ b/solution.py
@@ -5,6 +5,19 @@
 
 HEAD_DIM = 128
 blocked = -1e30
+
+
+def ring_gather(value, axis, dim):
+    devices, index, rows = (lax.axis_size(axis), lax.axis_index(axis), value.shape[dim])
+    ahead = [(i, (i + 1) % devices) for i in range(devices)]
+    out = jnp.zeros((*value.shape[:dim], devices * rows, *value.shape[dim + 1 :]), value.dtype)
+    carried = value
+    for hop in range(devices):
+        holder = (index - hop) % devices
+        out = lax.dynamic_update_slice_in_dim(out, carried, holder * rows, axis=dim)
+        if hop < devices - 1:
+            carried = lax.ppermute(carried, axis, ahead)
+    return out
 
 
 def split_heads(matrix):
@@ -23,7 +36,7 @@
     local_tokens = query_states.shape[0]
     query_heads = split_heads(query_states)
     local_heads = query_heads.shape[1]
-    all_keys = lax.all_gather(key_states, "seq", axis=0, tiled=True)
+    all_keys = ring_gather(key_states, "seq", 0)
     all_values = lax.all_gather(value_states, "seq", axis=0, tiled=True)
     all_pos = lax.all_gather(positions, "seq", axis=0, tiled=True)
     key_heads = split_heads(all_keys)

time: 489 us -> 461 us (0.943)
  waiting for transfers between devices: 316 us -> 259 us
  local copies, waits for them, and re-layouts: 25.2 us -> 38 us
  matrix products: 74.1 us -> 83.9 us
    ppermute x0 -> x7, waiting for transfers between devices: none -> 61.6 us  [ring_gather(): carried = lax.ppermute(carried, axis, ahead)]
    all_gather x1, waiting for transfers between devices: 45.4 us -> 0.01 us  [shards(): cotangent_full = lax.all_gather(cotangent, 'fsdp', axis=1, tiled=True)]
    all_gather x1 -> x0, waiting for transfers between devices: 33.3 us -> none  [shards(): all_keys = lax.all_gather(key_states, 'seq', axis=0, tiled=True)]
    all_gather x1, waiting for transfers between devices: 24.7 us -> 0.02 us  [shards(): all_values = lax.all_gather(value_states, 'seq', axis=0, tiled=True)]
    all_gather x1, waiting for transfers between devices: 63.5 us -> 49.1 us  [shards(): weight_full = lax.all_gather(out_weight, 'seq', axis=1, tiled=True)]
    dynamic_update_slice x0 -> x8, local copies, waits for them, and re-layouts: none -> 7.05 us  [ring_gather(): out = lax.dynamic_update_slice_in_dim(out, carried, holder * rows, axis=dim)]
    ppermute x0 -> x7, local copies, waits for them, and re-layouts: none -> 6.64 us  [ring_gather(): carried = lax.ppermute(carried, axis, ahead)]
    dot_general x1, matrix products: 5.27 us -> 11.1 us  [masked_scores(): jnp.einsum('qhd,khd->hqk', query_rows, key_rows, preferred_element_type=j...]
  transfers between devices with their start and end apart: 8 -> 14, of which waited for: 7 -> 10; matrix products, arithmetic and copies ran while one was open for 15% -> 22% of each run, Pallas kernels for 0% -> 0%
where the time goes in v1:
time: 461 us; the launch traced here: 460 us
  waiting for transfers between devices  259 us (56%)
  matrix products  83.9 us (18%)
  blocking collectives  50.3 us (11%)
  local copies, waits for them, and re-layouts  38 us (8%)
  between operations  14.5 us (3%)
  other arithmetic  13.2 us (3%)
    reduce_scatter x1, waiting for transfers between devices, shards(): lax.psum_scatter(value_part, 'seq', scatter_dimension=0, tiled=True)  71.8 us
    reduce_scatter x1, waiting for transfers between devices, shards(): key_sum = lax.psum_scatter(key_part, 'seq', scatter_dimension=0, tiled=True)  66.8 us
    ppermute x7, waiting for transfers between devices, ring_gather(): carried = lax.ppermute(carried, axis, ahead)  61.6 us
    all_gather x1, waiting for transfers between devices, shards(): weight_full = lax.all_gather(out_weight, 'seq', axis=1, tiled=True)  49.1 us
    all_to_all x1, blocking collectives, shards(): cotangent_cols = lax.all_to_all(cotangent_full, 'seq', 1, 0, tiled=True)  41.3 us
    dot_general x1, matrix products, shards(): jnp.einsum('hqk,qhd->khd', weights, grad_heads, preferred_element_type=jn...  13.6 us
    unnamed x19, local copies, waits for them, and re-layouts  11.8 us
    dot_general x1, matrix products, shards(): jnp.einsum('qhd,khd->hqk', grad_heads, value_heads, preferred_element_typ...  11.7 us
  transfers between devices with their start and end apart: 14, of which 10 were waited for; matrix products, arithmetic and copies ran while one was open for 22% of the time, Pallas kernels for 0%

profile of v1, /device:TPU:0, one launch (start us, length us, event | category | flops | bytes accessed | tf_op | source)
XLA Modules:
  0.0 459.8 jit_solution(17724602555356251132)
XLA Ops:
  8.0 2.2 copy.92
  11.5 9.9 %collective-permute-done = bf16[256,1024]{1,0:T(8,128)(2,1)S(1)} collective-permute-done((bf16[256,1024]{1,0:T(8,128)(2,1)}, bf16[256,1024]{1,0:T(8,128)(2,1)S(1)}, u32[]{:S(2)}, u32[]{:S(2)}) %collective-permute-start) | collective-permute-done | bytes 524320 | tf_op jit(solution)/shard_map/ppermute | solution.py:19
  21.4 13.5 %collective-permute-done.1 = bf16[256,1024]{1,0:T(8,128)(2,1)S(1)} collective-permute-done((bf16[256,1024]{1,0:T(8,128)(2,1)S(1)}, bf16[256,1024]{1,0:T(8,128)(2,1)S(1)}, u32[]{:S(2)}, u32[]{:S(2)}) %collective-permute-start.1) | collective-permute-done | bytes 524320 | tf_op jit(solution)/shard_map/ppermute | solution.py:19
  35.0 20.4 %collective-permute-done.2 = bf16[256,1024]{1,0:T(8,128)(2,1)S(1)} collective-permute-done((bf16[256,1024]{1,0:T(8,128)(2,1)S(1)}, bf16[256,1024]{1,0:T(8,128)(2,1)S(1)}, u32[]{:S(2)}, u32[]{:S(2)}) %collective-permute-start.2) | collective-permute-done | bytes 524320 | tf_op jit(solution)/shard_map/ppermute | solution.py:19
  55.4 9.5 %collective-permute-done.3 = bf16[256,1024]{1,0:T(8,128)(2,1)S(1)} collective-permute-done((bf16[256,1024]{1,0:T(8,128)(2,1)S(1)}, bf16[256,1024]{1,0:T(8,128)(2,1)S(1)}, u32[]{:S(2)}, u32[]{:S(2)}) %collective-permute-start.3) | collective-permute-done | bytes 524320 | tf_op jit(solution)/shard_map/ppermute | solution.py:19
  66.4 9.0 %all-gather = s32[8,1,256]{2,1,0:T(1,128)S(1)} all-gather(s32[1,1,256]{2,1,0:T(1,128)} %bitcast.78), channel_id=1, replica_groups=mesh['seq'=8,'fsdp'=4] {'seq'}, dimensions={0}, use_global_device_ids=true | all-gather | bytes 9216 | tf_op jit(solution)/shard_map/all_gather | solution.py:41
  75.3 2.5 broadcast_in_dim.21
  82.9 5.7 %collective-permute-done.5 = bf16[256,1024]{1,0:T(8,128)(2,1)} collective-permute-done((bf16[256,1024]{1,0:T(8,128)(2,1)}, bf16[256,1024]{1,0:T(8,128)(2,1)}, u32[]{:S(2)}, u32[]{:S(2)}) %collective-permute-start.5) | collective-permute-done | bytes 524320 | tf_op jit(solution)/shard_map/ppermute | solution.py:19
  95.9 2.5 collective-permute-done.6
  100.5 11.1 %fusion.1 = (f32[8,256]{1,0:T(8,128)S(1)}, f32[8,2048,256]{2,1,0:T(8,128)}) fusion(pred[256,2048]{0,1:T(8,128)(4,1)S(1)} %broadcast_compare_fusion, bf16[2048,8,128]{0,2,1:T(8,128)(2,1)} %bitcast.2, bf16[256,1024]{1,0:T(8,128)(2,1)S(1)} %copy-done), kind=kOutput, calls=%fused_computation.5 | convolution fusion | flops 1086322688 | bytes 22028288 | tf_op jit(solution)/shard_map/qhd,khd->hqk/dot_general | solution.py:28
  111.5 9.2 %exponential_reduce_fusion = f32[8,256]{1,0:T(8,128)S(1)} fusion(f32[8,2048,256]{2,1,0:T(8,128)} %get-tuple-element.26, f32[8,256]{1,0:T(8,128)S(1)} %get-tuple-element.25, pred[256,2048]{0,1:T(8,128)(4,1)S(1)} %broadcast_compare_fusion), kind=kLoop, calls=%fused_computation.3 | loop fusion | flops 16775168 | bytes 17317888 | tf_op jit(solution)/shard_map/reduce_sum | solution.py:46
  120.8 6.8 %copy.90 = bf16[2048,1024]{0,1:T(8,128)(2,1)} copy(bf16[2048,1024]{1,0:T(8,128)(2,1)} %all-gather.6.cloned.1.call-done) | data formatting | bytes 8388608 | tf_op jit(solution)/shard_map/all_gather | solution.py:40
  127.6 49.1 %all-gather.8.cloned.1.call-done = bf16[1024,5120]{1,0:T(8,128)(2,1)} async-done(((bf16[1024,640]{1,0:T(8,128)(2,1)}), bf16[1024,5120]{1,0:T(8,128)(2,1)}) %all-gather.8.cloned.1.call-update) | async-done | bytes 10485776 | tf_op jit(solution)/shard_map/all_gather | solution.py:52
  176.7 7.7 %convolution_convert_fusion.1 = bf16[256,1024]{1,0:T(8,128)(2,1)S(1)} fusion(bf16[256,5120]{0,1:T(8,128)(2,1)} %all-gather.10.cloned.1.call-done, bf16[1024,5120]{1,0:T(8,128)(2,1)} %all-gather.8.cloned.1.call-done), kind=kOutput, calls=%fused_computation.10 | convolution fusion | flops 2684616704 | bytes 13631488 | tf_op jit(solution)/shard_map/td,hd->th/dot_general | solution.py:60
  184.7 11.2 %multiply_reduce_fusion = (f32[256,8]{0,1:T(8,128)S(1)}, bf16[8,256,128]{1,2,0:T(8,128)(2,1)S(1)}) fusion(bf16[256,1024]{0,1:T(8,128)(2,1)S(1)} %copy.93, bf16[2048,8,128]{0,2,1:T(8,128)(2,1)} %bitcast.67, f32[8,2048,256]{2,1,0:T(8,128)} %get-tuple-element.26, f32[8,256]{1,0:T(8,128)S(1)} %log_add_fusion, pred[256,2048]{0,1:T(8,128)(4,1)S(1)} %broadcast_compare_fusion), kind=kOutput, calls=%fused_computation.12 | convolution fusion | flops 1091827712 | bytes 22560768 | tf_op jit(solution)/shard_map/hqk,khd->qhd/dot_general | solution.py:49
  195.9 8.4 %convolution_convert_fusion = bf16[256,5120]{1,0:T(8,128)(2,1)} fusion(bf16[256,1024]{0,1:T(8,128)(2,1)S(1)} %bitcast.70, bf16[1024,5120]{1,0:T(8,128)(2,1)} %all-gather.8.cloned.1.call-done), kind=kOutput, calls=%fused_computation.6 | convolution fusion | flops 2685665280 | bytes 13631488 | tf_op jit(solution)/shard_map/dot_general | solution.py:53
  205.0 11.7 %multiply_convert_fusion = bf16[8,256,2048]{1,2,0:T(8,128)(2,1)S(1)} fusion(f32[8,2048,256]{2,1,0:T(8,128)} %get-tuple-element.26, f32[8,256]{1,0:T(8,128)S(1)} %bitcast.79, f32[8,256]{1,0:T(8,128)S(1)} %log_add_fusion, pred[256,2048]{0,1:T(8,128)(4,1)S(1)} %broadcast_compare_fusion, bf16[256,8,128]{0,2,1:T(8,128)(2,1)S(1)} %bitcast.74, ...), kind=kOutput, calls=%fused_computation.1 | convolution fusion | flops 1098907648 | bytes 30425088 | tf_op jit(solution)/shard_map/qhd,khd->hqk/dot_general | solution.py:72
  216.7 3.2 copy-done.2
  219.9 5.6 %convolution_bitcast_fusion.1 = f32[2048,8,128]{2,0,1:T(8,128)} fusion(bf16[8,256,2048]{1,2,0:T(8,128)(2,1)S(1)} %multiply_convert_fusion, bf16[256,1024]{1,0:T(8,128)(2,1)S(1)} %copy-done), kind=kOutput, calls=%fused_computation.8 | convolution fusion | flops 1073741824 | bytes 17301504 | tf_op jit(solution)/shard_map/hqk,qhd->khd/dot_general | solution.py:79
  225.5 13.6 %convolution_bitcast_fusion = f32[2048,8,128]{0,2,1:T(8,128)} fusion(bf16[256,8,128]{0,2,1:T(8,128)(2,1)S(1)} %bitcast.75, f32[8,2048,256]{2,1,0:T(8,128)} %get-tuple-element.26, f32[8,256]{1,0:T(8,128)S(1)} %log_add_fusion, pred[256,2048]{0,1:T(8,128)(4,1)S(1)} %broadcast_compare_fusion), kind=kOutput, calls=%fused_computation.7 | convolution fusion | flops 1090519040 | bytes 26222592 | tf_op jit(solution)/shard_map/hqk,qhd->khd/dot_general | solution.py:82
  239.2 41.3 %all_to_all.19 = bf16[256,8,640]{0,2,1:T(8,128)(2,1)S(1)} all-to-all(bf16[256,8,640]{0,2,1:T(8,128)(2,1)} %bitcast.72), channel_id=1, replica_groups=mesh['seq'=8,'fsdp'=4] {'seq'}, dimensions={1} | all-to-all | bytes 5242880 | tf_op jit(solution)/shard_map/all_to_all | solution.py:64
  280.6 2.6 copy.101
  283.1 6.6 %convolution_multiply_fusion = f32[8,128,256]{2,1,0:T(8,128)S(1)} fusion(bf16[2048,8,128]{0,2,1:T(8,128)(2,1)} %bitcast.2, bf16[8,256,2048]{1,2,0:T(8,128)(2,1)} %copy-done.2), kind=kOutput, calls=%fused_computation.9 | convolution fusion | flops 1074003968 | bytes 13631488 | tf_op jit(solution)/shard_map/hqk,khd->qhd/dot_general | solution.py:76
  289.8 1.3 copy.102
  291.1 2.2 convert_element_type.31
  293.3 7.6 %all-gather.12.cloned.1.call-done = bf16[2048,1024]{0,1:T(8,128)(2,1)} async-done(((bf16[256,1024]{0,1:T(8,128)(2,1)}), bf16[2048,1024]{0,1:T(8,128)(2,1)}) %all-gather.12.cloned.1.call-update) | async-done | bytes 4194320 | tf_op jit(solution)/shard_map/all_gather | solution.py:63
  300.9 8.0 %fusion.9 = f32[1024,640]{1,0:T(8,128)} fusion(bf16[2048,1024]{0,1:T(8,128)(2,1)} %all-gather.12.cloned.1.call-done, bf16[2048,640]{1,0:T(8,128)(2,1)} %bitcast.73), kind=kOutput, calls=%fused_computation.29 | convolution fusion | flops 2684354560 | bytes 9437184 | tf_op jit(solution)/shard_map/th,td->hd/dot_general | solution.py:65
  308.9 66.8 %reduce-scatter.6.cloned.1.call-done = f32[256,8,128]{2,0,1:T(8,128)} async-done(((f32[2048,8,128]{2,0,1:T(8,128)}), f32[256,8,128]{2,0,1:T(8,128)}) %reduce-scatter.6.cloned.1.call-update) | async-done | bytes 1048592 | tf_op jit(solution)/shard_map/reduce_scatter | solution.py:83
  375.7 1.3 broadcast_multiply_fusion
  377.3 1.3 copy.103
  378.6 71.8 %reduce-scatter.8.cloned.1.call-done = f32[256,8,128]{0,2,1:T(8,128)} async-done(((f32[2048,8,128]{0,2,1:T(8,128)}), f32[256,8,128]{0,2,1:T(8,128)}) %reduce-scatter.8.cloned.1.call-update) | async-done | bytes 1048592 | tf_op jit(solution)/shard_map/reduce_scatter | solution.py:84
  450.5 2.5 copy.104
  (58 shorter events, 19.1 us)
Async XLA Ops:
  7.2 93.3 %copy-start = (bf16[256,1024]{1,0:T(8,128)(2,1)S(1)}, bf16[256,1024]{1,0:T(8,128)(2,1)}, u32[]{:S(2)}) copy-start(bf16[256,1024]{1,0:T(8,128)(2,1)} %param.6) | copy-start | bytes 1572868
  7.2 71.8 %copy-start.6 = (s32[256]{0:T(256)S(1)}, s32[256]{0:T(256)}, u32[]{:S(2)}) copy-start(s32[256]{0:T(256)} %param.9) | copy-start | bytes 3076
  7.2 113.6 %all-gather.6.cloned.1.call-start = ((), (), s32[]{:S(2)}) async-start(), calls=%async_computation.4 | async-start | bytes 4718592 | tf_op jit(solution)/shard_map/all_gather | solution.py:40
  7.9 119.7 %all-gather.10.cloned.1.call-start = ((), (), s32[]{:S(2)}) async-start(), calls=%async_computation.7 | async-start | bytes 3276800 | tf_op jit(solution)/shard_map/all_gather | solution.py:59
  10.2 166.6 %all-gather.8.cloned.1.call-start = ((), (), s32[]{:S(2)}) async-start(), calls=%async_computation.5 | async-start | bytes 11796480 | tf_op jit(solution)/shard_map/all_gather | solution.py:52
  10.9 280.2 %reduce-scatter.4.cloned.1.call-start = ((), (), s32[]{:S(2)}) async-start(), calls=%async_computation.6 | async-start | bytes 3276800 | tf_op jit(solution)/shard_map/reduce_scatter | solution.py:56
  10.9 10.5 %collective-permute-start = (bf16[256,1024]{1,0:T(8,128)(2,1)}, bf16[256,1024]{1,0:T(8,128)(2,1)S(1)}, u32[]{:S(2)}, u32[]{:S(2)}) collective-permute-start(bf16[256,1024]{1,0:T(8,128)(2,1)} %param.7), channel_id=1, source_target_pairs={{0,4},{4,8},{8,12},{12,16},{16,20},{20,24},{24,28},{28,0},{1,5},{5... | collective-permute-start | bytes 1572872 | tf_op jit(solution)/shard_map/ppermute | solution.py:19
  21.4 43.5 %copy-start.4 = (bf16[256,1024]{1,0:T(8,128)(2,1)}, bf16[256,1024]{1,0:T(8,128)(2,1)S(1)}, u32[]{:S(2)}) copy-start(bf16[256,1024]{1,0:T(8,128)(2,1)S(1)} %collective-permute-done) | copy-start | bytes 1572868
  21.4 13.5 %collective-permute-start.1 = (bf16[256,1024]{1,0:T(8,128)(2,1)S(1)}, bf16[256,1024]{1,0:T(8,128)(2,1)S(1)}, u32[]{:S(2)}, u32[]{:S(2)}) collective-permute-start(bf16[256,1024]{1,0:T(8,128)(2,1)S(1)} %collective-permute-done), channel_id=1, source_target_pairs={{0,4},{4,8},{8,12},{12,16},{16,20},{20,24},{24,28},{28,0},{1,5},{5... | collective-permute-start | bytes 1572872 | tf_op jit(solution)/shard_map/ppermute | solution.py:19
  35.0 29.9 %copy-start.5 = (bf16[256,1024]{1,0:T(8,128)(2,1)}, bf16[256,1024]{1,0:T(8,128)(2,1)S(1)}, u32[]{:S(2)}) copy-start(bf16[256,1024]{1,0:T(8,128)(2,1)S(1)} %collective-permute-done.1) | copy-start | bytes 1572868
  35.0 20.4 %collective-permute-start.2 = (bf16[256,1024]{1,0:T(8,128)(2,1)S(1)}, bf16[256,1024]{1,0:T(8,128)(2,1)S(1)}, u32[]{:S(2)}, u32[]{:S(2)}) collective-permute-start(bf16[256,1024]{1,0:T(8,128)(2,1)S(1)} %collective-permute-done.1), channel_id=1, source_target_pairs={{0,4},{4,8},{8,12},{12,16},{16,20},{20,24},{24,28},{28,0},{1,5},{5... | collective-permute-start | bytes 1572872 | tf_op jit(solution)/shard_map/ppermute | solution.py:19
  55.4 9.5 %collective-permute-start.3 = (bf16[256,1024]{1,0:T(8,128)(2,1)S(1)}, bf16[256,1024]{1,0:T(8,128)(2,1)S(1)}, u32[]{:S(2)}, u32[]{:S(2)}) collective-permute-start(bf16[256,1024]{1,0:T(8,128)(2,1)S(1)} %collective-permute-done.2), channel_id=1, source_target_pairs={{0,4},{4,8},{8,12},{12,16},{16,20},{20,24},{24,28},{28,0},{1,5},{5... | collective-permute-start | bytes 1572872 | tf_op jit(solution)/shard_map/ppermute | solution.py:19
  64.9 13.8 %collective-permute-start.4 = (bf16[256,1024]{1,0:T(8,128)(2,1)S(1)}, bf16[256,1024]{1,0:T(8,128)(2,1)}, u32[]{:S(2)}, u32[]{:S(2)}) collective-permute-start(bf16[256,1024]{1,0:T(8,128)(2,1)S(1)} %collective-permute-done.3), channel_id=1, source_target_pairs={{0,4},{4,8},{8,12},{12,16},{16,20},{20,24},{24,28},{28,0},{1,5},{5... | collective-permute-start | bytes 1572872 | tf_op jit(solution)/shard_map/ppermute | solution.py:19
  78.7 9.8 %collective-permute-start.5 = (bf16[256,1024]{1,0:T(8,128)(2,1)}, bf16[256,1024]{1,0:T(8,128)(2,1)}, u32[]{:S(2)}, u32[]{:S(2)}) collective-permute-start(bf16[256,1024]{1,0:T(8,128)(2,1)} %collective-permute-done.4), channel_id=1, source_target_pairs={{0,4},{4,8},{8,12},{12,16},{16,20},{20,24},{24,28},{28,0},{1,5},{5... | collective-permute-start | bytes 1572872 | tf_op jit(solution)/shard_map/ppermute | solution.py:19
  88.5 9.8 %collective-permute-start.6 = (bf16[256,1024]{1,0:T(8,128)(2,1)}, bf16[256,1024]{1,0:T(8,128)(2,1)}, u32[]{:S(2)}, u32[]{:S(2)}) collective-permute-start(bf16[256,1024]{1,0:T(8,128)(2,1)} %collective-permute-done.5), channel_id=1, source_target_pairs={{0,4},{4,8},{8,12},{12,16},{16,20},{20,24},{24,28},{28,0},{1,5},{5... | collective-permute-start | bytes 1572872 | tf_op jit(solution)/shard_map/ppermute | solution.py:19
  195.9 8.4 %copy-start.3 = (bf16[8,256,128]{1,2,0:T(8,128)(2,1)}, bf16[8,256,128]{1,2,0:T(8,128)(2,1)S(1)}, u32[]{:S(2)}) copy-start(bf16[8,256,128]{1,2,0:T(8,128)(2,1)S(1)} %get-tuple-element.28) | copy-start | bytes 1572868
  204.3 96.6 %all-gather.12.cloned.1.call-start = ((), (), s32[]{:S(2)}) async-start(), calls=%async_computation.10 | async-start | bytes 4718592 | tf_op jit(solution)/shard_map/all_gather | solution.py:63
  204.9 170.7 %reduce-scatter.6.cloned.1.call-start = ((), (), s32[]{:S(2)}) async-start(), calls=%async_computation.8 | async-start | bytes 9437184 | tf_op jit(solution)/shard_map/reduce_scatter | solution.py:83
  216.7 3.2 copy-start.2
  225.5 225.0 %reduce-scatter.8.cloned.1.call-start = ((), (), s32[]{:S(2)}) async-start(), calls=%async_computation.9 | async-start | bytes 9437184 | tf_op jit(solution)/shard_map/reduce_scatter | solution.py:84
  300.9 152.0 %copy-start.1 = (bf16[256,1024]{1,0:T(8,128)(2,1)S(1)}, bf16[256,1024]{1,0:T(8,128)(2,1)}, u32[]{:S(2)}) copy-start(bf16[256,1024]{1,0:T(8,128)(2,1)} %param.6) | copy-start | bytes 1572868
Sparse Core Ops, SparseCore 0:
  9.9 46.1 all-gather.5
  58.2 54.8 all-gather.9
  114.9 61.7 all-gather.7
  204.4 52.2 reduce-scatter.3
  259.0 41.8 all-gather.11
  304.3 71.3 reduce-scatter.5
  379.1 71.2 reduce-scatter.7
